TPU v7x, 256 devices: a whole 4x4x8 slice. The times are simulated.
256 devices in a mesh: section: 4 (over z_lo, core), seq: 64 (over y, x, z_hi).
Axes of the slice: x: 4, y: 4, z: 8 (z_hi: 4, z_lo: 2; z = z_hi * 2 + z_lo), core: 2. Of those that a mesh axis runs over, the one named last changes fastest.
Arguments:
- q_img: bfloat16 [8192, 3072], P('seq', 'section'), may hold values from -6 to 6
- k_img: bfloat16 [8192, 3072], P('seq', 'section'), may hold values from -6 to 6
- v_img: bfloat16 [8192, 3072], P('seq', 'section'), may hold values from -6 to 6
- q_txt: bfloat16 [256, 3072], P('seq', 'section'), may hold values from -6 to 6
- k_txt: bfloat16 [256, 3072], P('seq', 'section'), may hold values from -6 to 6
- v_txt: bfloat16 [256, 3072], P('seq', 'section'), may hold values from -6 to 6
- norm_gains: float32 [4, 128], replicated, may hold values from 1.2 to 2
- block_map: int32 [24, 64, 64], P('section', 'seq'), may hold values 0 or 1
Outputs:
- image_out: bfloat16 [2048, 4, 3072], P('seq', 'section')
- text_out: bfloat16 [256, 3072], P('seq', 'section')
All inputs are finite; a program needn't handle non-finite values. No bound on the sum of `block_map` on one device may be relied on, other than what follows from the above.
Results may differ from a plain program's by a relative error of at most 0.011.
Values may be sent and summed in bfloat16 or wider, within the bound.
No kernel may reach another device: no remote copies, remote signals or barrier semaphores. Data moves between devices by JAX's collectives and lax.ppermute only.
A program may use at most 256 MiB of HBM per device.

v0:
```python
import jax
import jax.numpy as jnp
from jax import lax
from jax.sharding import PartitionSpec as P

BLOCK = 128


def normed(values, gain, heads):
    rows = values.shape[0]
    floats = values.astype(jnp.float32).reshape(rows, heads, gain.shape[0])
    power = jnp.mean(floats * floats, axis=-1, keepdims=True)
    return (floats * lax.rsqrt(power + 1e-06) * gain).astype(jnp.bfloat16)


def make_keep(flags, query_shards, shards, first, rows, text_rows):
    heads = flags.shape[0]
    key_blocks = rows // BLOCK
    stride = rows + text_rows
    picked = lax.dynamic_slice_in_dim(flags, first * key_blocks, shards * key_blocks, 2)
    picked = picked.reshape(heads, query_shards, key_blocks, shards, key_blocks)
    image_mask = jnp.broadcast_to(
        picked[:, :, :, None, :, :, None] > 0,
        (heads, query_shards, key_blocks, BLOCK, shards, key_blocks, BLOCK),
    )
    image_mask = image_mask.reshape(heads, query_shards, rows, shards, rows)
    keep = jnp.pad(
        image_mask, ((0, 0), (0, 0), (0, text_rows), (0, 0), (0, text_rows)), constant_values=True
    )
    return keep.reshape(heads, query_shards * stride, shards, stride)


def accumulate(queries, flags, query_shards, rows, text_rows, carry, pieces, start):
    numer, denom = carry
    piece_keys, piece_values = pieces
    heads = queries.shape[1]
    head_size = queries.shape[2]
    stride = rows + text_rows
    shards = piece_keys.shape[0] // stride
    first = start // stride
    keys_four = piece_keys.reshape(shards, stride, heads, head_size)
    values_four = piece_values.reshape(shards, stride, heads, head_size)
    scores = jnp.einsum(
        "qhd,skhd->hqsk", queries, keys_four, preferred_element_type=jnp.float32
    ) * head_size ** (-0.5)
    keep = make_keep(flags, query_shards, shards, first, rows, text_rows)
    weights = jnp.where(keep, jnp.exp(scores), jnp.float32(0.0))
    denom = denom + jnp.sum(weights, axis=(2, 3))
    numer = numer + jnp.einsum(
        "hqsk,skhd->hqd",
        weights.astype(jnp.bfloat16),
        values_four,
        preferred_element_type=jnp.float32,
    )
    return (numer, denom)


def body(q_img, k_img, v_img, q_txt, k_txt, v_txt, norm_gains, block_map):
    rows, width = q_img.shape
    head_size = norm_gains.shape[1]
    heads = width // head_size
    text_rows = q_txt.shape[0]
    stride = rows + text_rows
    queries = jnp.concatenate(
        [normed(q_img, norm_gains[0], heads), normed(q_txt, norm_gains[2], heads)], axis=0
    )
    keys_image = normed(k_img, norm_gains[1], heads).reshape(rows, width)
    keys_text = normed(k_txt, norm_gains[3], heads).reshape(text_rows, width)
    local_keys = jnp.concatenate([keys_image, keys_text], axis=0)
    local_values = jnp.concatenate([v_img, v_txt], axis=0)
    start_state = (
        jnp.zeros((heads, stride, head_size), jnp.float32),
        jnp.zeros((heads, stride), jnp.float32),
    )

    def fold_step(carry, pieces, start):
        return accumulate(queries, block_map, 1, rows, text_rows, carry, pieces, start)

    whole_keys, whole_values = (
        lax.all_gather(local_keys, "seq", axis=0, tiled=True),
        lax.all_gather(local_values, "seq", axis=0, tiled=True),
    )
    count_seq = lax.axis_size("seq")
    grouped = 1
    while (
        grouped * 2 <= count_seq
        and count_seq % (grouped * 2) == 0
        and (grouped * 2 * stride <= 1024)
    ):
        grouped = grouped * 2
    span = grouped * stride

    def step_over(index, carry):
        offset = index * span
        piece_keys = lax.dynamic_slice_in_dim(whole_keys, offset, span, 0)
        piece_values = lax.dynamic_slice_in_dim(whole_values, offset, span, 0)
        return fold_step(carry, (piece_keys, piece_values), offset)

    numer, denom = lax.fori_loop(0, count_seq // grouped, step_over, start_state)
    result = numer / denom[..., None]
    merged = result.transpose(1, 0, 2).reshape(stride, width).astype(jnp.bfloat16)
    image_part = merged[:rows]
    text_out = merged[rows:]
    sections = lax.axis_size("section")
    image_out = lax.all_to_all(
        image_part.reshape(rows // sections, sections, width),
        "section",
        split_axis=1,
        concat_axis=2,
        tiled=True,
    )
    return (image_out, text_out)


def solution(mesh):
    placed = (
        P("seq", "section"),
        P("seq", "section"),
        P("seq", "section"),
        P("seq", "section"),
        P("seq", "section"),
        P("seq", "section"),
        P(),
        P("section", "seq", None),
    )
    return jax.shard_map(
        body,
        mesh=mesh,
        in_specs=placed,
        out_specs=(P("seq", "section", None), P("seq", "section")),
        check_vma=False,
    )
```

profile of v0, /device:TPU:4, one launch (start us, length us, event | category | flops | bytes accessed | tf_op | source)
XLA Modules:
  0.0 707.3 jit_solution(929896019080219932)
XLA Ops:
  14.1 136.7 %all-gather.5.cloned.1.call-done = bf16[64,132,768]{2,1,0:T(8,128)(2,1)} async-done(((bf16[1,132,768]{2,1,0:T(8,128)(2,1)}), bf16[64,132,768]{2,1,0:T(8,128)(2,1)}) %all-gather.5.cloned.1.call-update) | async-done | bytes 12976144 | tf_op jit(solution)/shard_map/all_gather | solution.py:80
  150.8 16.0 %reshape.141 = bf16[8448,768]{1,0:T(8,128)(2,1)} reshape(bf16[64,132,768]{2,1,0:T(8,128)(2,1)} %all-gather.5.cloned.1.call-done) | data formatting | bytes 25952256
  166.8 131.9 %all-gather.7.cloned.1.call-done = bf16[64,132,768]{2,1,0:T(8,128)(2,1)} async-done(((bf16[1,132,768]{2,1,0:T(8,128)(2,1)}), bf16[64,132,768]{2,1,0:T(8,128)(2,1)}) %all-gather.7.cloned.1.call-update) | async-done | bytes 12976144 | tf_op jit(solution)/shard_map/all_gather | solution.py:81
  298.7 16.1 %reshape.143 = bf16[8448,768]{1,0:T(8,128)(2,1)} reshape(bf16[64,132,768]{2,1,0:T(8,128)(2,1)} %all-gather.7.cloned.1.call-done) | data formatting | bytes 25952256
  314.8 363.8 %while.18 = (s32[]{:T(128)}, f32[6,132,128]{2,1,0:T(8,128)}, f32[6,132]{1,0:T(8,128)S(1)}, s32[6,1,64]{0,2,1:T(8,128)S(1)}, bf16[8448,768]{1,0:T(8,128)(2,1)}, /...) while((s32[]{:T(128)}, f32[6,132,128]{2,1,0:T(8,128)}, ...), condition=%wide.region_6.7_spmd.clone, body=%wide.region_4.6_spmd.clone.sunk | while | flops 215982384 | bytes 21925776 | solution.py:99
  321.6 4.7 copy.123
  344.2 4.7 copy.123
  354.9 3.3 fusion.36
  367.0 4.7 copy.123
  377.6 3.3 fusion.36
  389.7 4.7 copy.123
  412.5 4.7 copy.123
  435.2 4.7 copy.123
  445.9 3.3 fusion.36
  458.0 4.7 copy.123
  480.7 4.7 copy.123
  491.4 3.3 fusion.36
  503.5 4.7 copy.123
  514.1 3.3 fusion.36
  526.2 4.7 copy.123
  549.0 4.7 copy.123
  559.6 3.3 fusion.36
  571.7 4.7 copy.123
  582.3 3.3 fusion.36
  594.4 4.7 copy.123
  617.2 4.7 copy.123
  627.8 3.3 fusion.36
  639.9 4.7 copy.123
  650.6 3.3 fusion.36
  662.7 4.7 copy.123
  680.8 13.4 %all-to-all-start = ((bf16[32,4,768]{2,0,1:T(8,128)(2,1)}), bf16[32,4,768]{2,0,1:T(8,128)(2,1)S(1)}, u32[]{:S(2)}, u32[]{:S(2)}) async-start(bf16[32,4,768]{2,0,1:T(8,128)(2,1)} %copy.97), calls=%async_computation | async-start | bytes 393216 | tf_op jit(solution)/shard_map/all_to_all | solution.py:105
  694.7 4.7 all-to-all-done
  (251 shorter events, 268.2 us)
Async XLA Ops:
  7.2 5.1 copy-start.1
  7.2 5.1 copy-start.3
  7.2 5.8 copy-start.4
  7.2 6.0 copy-start.2
  7.2 143.6 %all-gather.5.cloned.1.call-start = ((), (), s32[]{:S(2)}) async-start(), calls=%async_computation.1 | async-start | bytes 13578240 | tf_op jit(solution)/shard_map/all_gather | solution.py:80
  11.1 2.9 copy-start.5
  12.2 286.5 %all-gather.7.cloned.1.call-start = ((), (), s32[]{:S(2)}) async-start(), calls=%async_computation.2 | async-start | bytes 13578240 | tf_op jit(solution)/shard_map/all_gather | solution.py:81
  332.2 3.2 copy-start
  354.9 3.3 copy-start
  377.6 3.3 copy-start
  400.4 3.3 copy-start
  423.1 3.3 copy-start
  445.9 3.3 copy-start
  468.6 3.3 copy-start
  491.4 3.3 copy-start
  514.1 3.3 copy-start
  536.9 3.3 copy-start
  559.6 3.3 copy-start
  582.3 3.3 copy-start
  605.1 3.3 copy-start
  627.8 3.3 copy-start
  650.6 3.3 copy-start
  673.3 3.3 copy-start
  680.8 18.7 %all-to-all-start = ((bf16[32,4,768]{2,0,1:T(8,128)(2,1)}), bf16[32,4,768]{2,0,1:T(8,128)(2,1)S(1)}, u32[]{:S(2)}, u32[]{:S(2)}) async-start(bf16[32,4,768]{2,0,1:T(8,128)(2,1)} %copy.97), calls=%async_computation | async-start | bytes 393216 | tf_op jit(solution)/shard_map/all_to_all | solution.py:105
Sparse Core Ops, SparseCore 0:
  12.3 138.4 all-gather.4
  154.1 144.5 all-gather.6
where the time goes:
time: 711 us; the launch traced here: 707 us
  waiting for transfers between devices  273 us (38%)
  local copies, waits for them, and re-layouts  229 us (32%)
  matrix products  89.9 us (13%)
  other arithmetic  86 us (12%)
  between operations  14.3 us (2%)
  starting transfers between devices  13.5 us (2%)
    all_gather x1, waiting for transfers between devices, body(): lax.all_gather(local_keys, 'seq', axis=0, tiled=True)  137 us
    all_gather x1, waiting for transfers between devices, body(): lax.all_gather(local_values, 'seq', axis=0, tiled=True)  132 us
    while x48, local copies, waits for them, and re-layouts  75.5 us
    dot_general x16, matrix products, accumulate(): jnp.einsum('hqsk,skhd->hqd', weights.astype(jnp.bfloat16), values_four, p...  52.2 us
    convert_element_type x16, other arithmetic, accumulate(): weights.astype(jnp.bfloat16)  50.4 us
    reshape x16, local copies, waits for them, and re-layouts, accumulate(): values_four = piece_values.reshape(shards, stride, heads, head_size)  44.4 us
    dynamic_slice x16, local copies, waits for them, and re-layouts, step_over(): piece_values = lax.dynamic_slice_in_dim(whole_values, offset, span, 0)  38.4 us
    dot_general x16, matrix products, accumulate(): jnp.einsum('qhd,skhd->hqsk', queries, keys_four, preferred_element_type=j...  37.6 us
  transfers between devices with their start and end apart: 3, of which 3 were waited for; matrix products, arithmetic and copies ran while one was open for 3% of the time, Pallas kernels for 0%

commit v1 on v0

--- a/solution.py
+++ b/solution.py
@@ -78,7 +78,9 @@
 
     whole_keys, whole_values = (
         lax.all_gather(local_keys, "seq", axis=0, tiled=True),
-        lax.all_gather(local_values, "seq", axis=0, tiled=True),
+        jnp.concatenate(
+            lax.all_to_all(jnp.stack([local_values] * lax.axis_size("seq")), "seq", 0, 0), axis=0
+        ),
     )
     count_seq = lax.axis_size("seq")
     grouped = 1

time: 711 us -> 843 us (1.19); the launches traced: 707 us -> 829 us
  waiting for transfers between devices: 273 us -> 385 us
    all_gather x1, waiting for transfers between devices: 137 us -> 380 us  [body(): lax.all_gather(local_keys, 'seq', axis=0, tiled=True)]
    all_gather x1 -> x0, waiting for transfers between devices: 132 us -> none  [body(): lax.all_gather(local_values, 'seq', axis=0, tiled=True)]
    reshape x0 -> x1, local copies, waits for them, and re-layouts: none -> 16.1 us  [body(): jnp.concatenate(lax.all_to_all(jnp.stack([local_values] * lax.axis_size('...]
    unnamed x18 -> x17, local copies, waits for them, and re-layouts: 34.6 us -> 18.5 us
    all_to_all x0 -> x1, starting transfers between devices: none -> 14.9 us  [body(): lax.all_to_all(jnp.stack([local_values] * lax.axis_size('seq')), 'seq', 0...]
    all_to_all x1, starting transfers between devices: 13.4 us -> 4.53 us  [body(): lax.all_to_all(image_part.reshape(rows // sections, sections, width), 'se...]
  transfers between devices with their start and end apart: 3 -> 3, of which waited for: 3 -> 2; matrix products, arithmetic and copies ran while one was open for 3% -> 3% of each run, Pallas kernels for 0% -> 0%
where the time goes in v1:
time: 843 us; the launch traced here: 829 us
  waiting for transfers between devices  385 us (46%)
  local copies, waits for them, and re-layouts  235 us (28%)
  matrix products  89.3 us (11%)
  other arithmetic  85.4 us (10%)
  starting transfers between devices  19.5 us (2%)
  between operations  14.3 us (2%)
    all_gather x1, waiting for transfers between devices, body(): lax.all_gather(local_keys, 'seq', axis=0, tiled=True)  380 us
    while x48, local copies, waits for them, and re-layouts  75.5 us
    dot_general x16, matrix products, accumulate(): jnp.einsum('hqsk,skhd->hqd', weights.astype(jnp.bfloat16), values_four, p...  51.9 us
    convert_element_type x16, other arithmetic, accumulate(): weights.astype(jnp.bfloat16)  50.4 us
    reshape x16, local copies, waits for them, and re-layouts, accumulate(): values_four = piece_values.reshape(shards, stride, heads, head_size)  44.4 us
    dynamic_slice x16, local copies, waits for them, and re-layouts, step_over(): piece_values = lax.dynamic_slice_in_dim(whole_values, offset, span, 0)  38.5 us
    dot_general x16, matrix products, accumulate(): jnp.einsum('qhd,skhd->hqsk', queries, keys_four, preferred_element_type=j...  37.4 us
    reduce_sum x16, other arithmetic, accumulate(): denom = denom + jnp.sum(weights, axis=(2, 3))  31.2 us
  transfers between devices with their start and end apart: 3, of which 2 were waited for; matrix products, arithmetic and copies ran while one was open for 3% of the time, Pallas kernels for 0%

profile of v1, /device:TPU:4, one launch (start us, length us, event | category | flops | bytes accessed | tf_op | source)
XLA Modules:
  0.0 829.3 jit_solution(11356613401572251958)
XLA Ops:
  12.2 5.6 stack.2
  17.8 14.9 %all-to-all-start = ((bf16[64,132,768]{2,1,0:T(8,128)(2,1)}), bf16[64,132,768]{2,1,0:T(8,128)(2,1)}, u32[]{:S(2)}, u32[]{:S(2)}) async-start(bf16[64,132,768]{2,1,0:T(8,128)(2,1)} %stack.2), calls=%async_computation | async-start | bytes 26738688 | tf_op jit(solution)/shard_map/all_to_all | solution.py:82
  33.9 380.0 %all-gather.3.cloned.1.call-done = bf16[64,132,768]{2,1,0:T(8,128)(2,1)} async-done(((bf16[1,132,768]{2,1,0:T(8,128)(2,1)}), bf16[64,132,768]{2,1,0:T(8,128)(2,1)}) %all-gather.3.cloned.1.call-update) | async-done | bytes 12976144 | tf_op jit(solution)/shard_map/all_gather | solution.py:80
  413.9 16.1 %reshape.147 = bf16[8448,768]{1,0:T(8,128)(2,1)} reshape(bf16[64,132,768]{2,1,0:T(8,128)(2,1)} %all-gather.3.cloned.1.call-done) | data formatting | bytes 25952256
  429.9 16.1 %reshape.140 = bf16[8448,768]{1,0:T(8,128)(2,1)} reshape(bf16[64,132,768]{2,1,0:T(8,128)(2,1)} %all-to-all-done) | data formatting | bytes 25952256 | tf_op jit(solution)/shard_map/reshape | solution.py:81
  446.1 363.4 %while.18 = (s32[]{:T(128)}, f32[6,132,128]{2,1,0:T(8,128)}, f32[6,132]{1,0:T(8,128)S(1)}, s32[6,1,64]{0,2,1:T(8,128)S(1)}, bf16[8448,768]{1,0:T(8,128)(2,1)}, /...) while((s32[]{:T(128)}, f32[6,132,128]{2,1,0:T(8,128)}, ...), condition=%wide.region_6.7_spmd.clone, body=%wide.region_4.6_spmd.clone.sunk | while | flops 215982384 | bytes 21925776 | solution.py:101
  452.9 4.7 copy.123
  475.5 4.7 copy.123
  486.1 3.2 fusion.36
  498.2 4.7 copy.123
  508.9 3.2 fusion.36
  520.9 4.7 copy.123
  531.6 3.2 fusion.36
  543.7 4.7 copy.123
  554.3 3.2 fusion.36
  566.4 4.7 copy.123
  577.0 3.2 fusion.36
  589.1 4.7 copy.123
  599.7 3.2 fusion.36
  611.8 4.7 copy.123
  622.5 3.2 fusion.36
  634.5 4.7 copy.123
  645.2 3.2 fusion.36
  657.3 4.7 copy.123
  680.0 4.7 copy.123
  702.7 4.7 copy.123
  725.4 4.7 copy.123
  748.1 4.7 copy.123
  770.9 4.7 copy.123
  793.6 4.7 copy.123
  811.6 4.5 all-to-all-start.1
  816.8 4.7 all-to-all-done.1
  (251 shorter events, 270.5 us)
Async XLA Ops:
  7.2 5.0 copy-start.1
  7.2 5.0 copy-start.3
  7.2 406.7 %all-gather.3.cloned.1.call-start = ((), (), s32[]{:S(2)}) async-start(), calls=%async_computation.2 | async-start | bytes 13578240 | tf_op jit(solution)/shard_map/all_gather | solution.py:80
  17.8 15.0 %copy-start.4 = (bf16[4,768]{1,0:T(4,128)(2,1)S(1)}, bf16[4,768]{1,0:T(4,128)(2,1)}, u32[]{:S(2)}) copy-start(bf16[4,768]{1,0:T(4,128)(2,1)} %param.13) | copy-start | bytes 18436
  17.8 15.1 %copy-start.2 = (bf16[128,768]{1,0:T(8,128)(2,1)S(1)}, bf16[128,768]{1,0:T(8,128)(2,1)}, u32[]{:S(2)}) copy-start(bf16[128,768]{1,0:T(8,128)(2,1)} %param.10) | copy-start | bytes 589828
  17.8 412.1 %all-to-all-start = ((bf16[64,132,768]{2,1,0:T(8,128)(2,1)}), bf16[64,132,768]{2,1,0:T(8,128)(2,1)}, u32[]{:S(2)}, u32[]{:S(2)}) async-start(bf16[64,132,768]{2,1,0:T(8,128)(2,1)} %stack.2), calls=%async_computation | async-start | bytes 26738688 | tf_op jit(solution)/shard_map/all_to_all | solution.py:82
  32.7 1.0 copy-start.5
  463.5 3.2 copy-start
  486.1 3.3 copy-start
  508.9 3.3 copy-start
  531.6 3.3 copy-start
  554.3 3.3 copy-start
  577.0 3.3 copy-start
  599.7 3.3 copy-start
  622.5 3.3 copy-start
  645.2 3.3 copy-start
  667.9 3.3 copy-start
  690.6 3.3 copy-start
  713.3 3.3 copy-start
  736.1 3.3 copy-start
  758.8 3.3 copy-start
  781.5 3.3 copy-start
  804.2 3.3 copy-start
  811.6 9.8 %all-to-all-start.1 = ((bf16[32,4,768]{2,0,1:T(8,128)(2,1)}), bf16[32,4,768]{2,0,1:T(8,128)(2,1)S(1)}, u32[]{:S(2)}, u32[]{:S(2)}) async-start(bf16[32,4,768]{2,0,1:T(8,128)(2,1)} %copy.97), calls=%async_computation.1 | async-start | bytes 393216 | tf_op jit(solution)/shard_map/all_to_all | solution.py:107
Sparse Core Ops, SparseCore 0:
  12.3 401.5 all-gather.2
